TPU v7x, 512 devices: a whole 4x8x8 slice. The times are simulated.
512 devices in a mesh: grp: 16 (over z, core), tok: 32 (over y, x).
Axes of the slice: x: 4, y: 8, z: 8, core: 2. Of those that a mesh axis runs over, the one named last changes fastest.
Arguments:
- patches: bfloat16 [32, 256, 1664], P('tok', 'grp'), may hold values from -54 to 54
- segment_ids: int32 [32, 256], P('tok'), may hold values from 0 to 32, as said below
- padding: int32 [32, 256], P('tok'), may hold values from 0 to 1, as said below
- request_owner: int32 [32, 32], P('tok'), may hold values from 0 to 31, as said below
- first_gain: float32 [1664], replicated, may hold values from 0.5 to 1.5
- first_shift: float32 [1664], replicated, may hold values from -3 to 3
- input_weight: bfloat16 [1664, 16, 312], P(None, 'grp'), may hold values from -0.15625 to 0.15625
- input_shift: float32 [16, 312], P('grp'), may hold values from -40 to 40
- output_weight: bfloat16 [16, 104, 1664], P('grp'), may hold values from -0.15625 to 0.15625
- output_shift: float32 [1664], replicated, may hold values from -3 to 3
- second_gain: float32 [1664], replicated, may hold values from 0.5 to 1.5
- second_shift: float32 [1664], replicated, may hold values from -3 to 3
- up_weight: bfloat16 [1664, 4096], P(None, 'grp'), may hold values from -0.15625 to 0.15625
- up_shift: float32 [4096], P('grp'), may hold values from -3 to 3
- down_weight: bfloat16 [4096, 1664], P('grp'), may hold values from -0.09375 to 0.09375
- down_shift: float32 [1664], replicated, may hold values from -3 to 3
- merge_weight: bfloat16 [6656, 1664], P(None, 'grp'), may hold values from -0.078125 to 0.078125
- merge_shift: float32 [1664], P('grp'), may hold values from -3 to 3
Outputs:
- routed: bfloat16 [32, 32, 8, 1664], P('tok', None, None, 'grp')
Inputs may be any that keep to these rules, and one draw needn't show every extreme that they name: `segment_ids`: patches come in aligned runs of four with one id (a 2x2 window); ids never fall along a group; an image spans 1 to 8 windows; every group holds an image of exactly 8 windows; padding stands at the end of a group and carries the id 32. `padding`: 0 exactly where segment_ids is 32. `request_owner`: every row is a permutation of 0 to 31; in every draw one owner receives an image of 8 windows from every group.
All inputs are finite; a program needn't handle non-finite values.
Results may differ from a plain program's by a relative error of at most 0.02.
The roundings to bfloat16 on the way count: a program that leaves them out, or rounds other values in their place, can miss the bound.
Values may be sent and summed in bfloat16 or wider, within the bound.
No kernel may reach another device: no remote copies, remote signals or barrier semaphores. Data moves between devices by JAX's collectives and lax.ppermute only.
A program may use at most 64 MiB of HBM per device.

v0:
```python
import jax
import jax.numpy as jnp
from jax import lax
from jax.sharding import PartitionSpec as P

CAP = 8
epsilon = 1e-06


def normalize(stream, factor, adjust):
    average = jnp.mean(stream, axis=-1, keepdims=True)
    centered = stream - average
    variance = jnp.mean(centered * centered, axis=-1, keepdims=True)
    return centered * lax.rsqrt(variance + epsilon) * factor + adjust


def attention_mask(segments, live_rows):
    count = segments.shape[0]
    same_image = segments[:, None] == segments[None, :]
    allowed = jnp.logical_and(same_image, live_rows[None, :] == 1)
    diagonal = jnp.arange(count)[:, None] == jnp.arange(count)[None, :]
    return jnp.logical_or(allowed, diagonal)


def softmax_rows(scores, allowed):
    masked = jnp.where(allowed, scores, -jnp.inf)
    row_max = jnp.max(masked, axis=-1, keepdims=True)
    powered = jnp.where(allowed, jnp.exp(masked - row_max), 0.0)
    return powered / jnp.sum(powered, axis=-1, keepdims=True)


def attend(projected, segments, live_rows, head_dim):
    queries = projected[:, :, :head_dim]
    key_rows = projected[:, :, head_dim : 2 * head_dim]
    value_rows = projected[:, :, 2 * head_dim :]
    scores = jnp.einsum(
        "qhe,khe->hqk", queries, key_rows, preferred_element_type=jnp.float32
    ) * head_dim ** (-0.5)
    probabilities = lax.optimization_barrier(
        softmax_rows(scores, attention_mask(segments, live_rows)[None]).astype(jnp.bfloat16)
    )
    return jnp.einsum(
        "hqk,khe->qhe", probabilities, value_rows, preferred_element_type=jnp.float32
    ).astype(jnp.bfloat16)


def summed_apart(terms):
    shards = lax.psum(1, "grp")
    rows = terms.shape[0] // shards
    pieces = lax.all_to_all(terms.reshape(shards, rows, terms.shape[1]), "grp", 0, 0, tiled=False)
    return jnp.sum(pieces.astype(jnp.float32), axis=0)


def routed_rows(merged, segments, live_rows, owners):
    window_segments = segments[::4]
    window_live = live_rows[::4]
    window_count = window_segments.shape[0]
    places = jnp.arange(window_count)
    earlier = jnp.logical_and(
        window_segments[None, :] == window_segments[:, None], places[None, :] < places[:, None]
    )
    slot_index = jnp.sum(earlier.astype(jnp.int32), axis=1)
    groups = owners.shape[0]
    matched = (jnp.arange(groups)[None, :] == window_segments[:, None]).astype(jnp.int32)
    owner_of = jnp.sum(matched * owners[None, :], axis=1)
    target = owner_of * CAP + slot_index
    one_hot = jnp.logical_and(
        target[:, None] == jnp.arange(groups * CAP)[None, :], window_live[:, None] == 1
    )
    outgoing = jnp.einsum(
        "wc,wd->cd", one_hot.astype(jnp.bfloat16), merged, preferred_element_type=jnp.float32
    )
    return outgoing.astype(jnp.bfloat16).reshape(groups, CAP, merged.shape[1])


def on_device(
    patches,
    segment_ids,
    padding,
    request_owner,
    first_gain,
    first_shift,
    input_weight,
    input_shift,
    output_weight,
    output_shift,
    second_gain,
    second_shift,
    up_weight,
    up_shift,
    down_weight,
    down_shift,
    merge_weight,
    merge_shift,
):
    row_count = patches.shape[1]
    model_width = patches.shape[2]
    head_dim = input_weight.shape[2] // 3
    segments = segment_ids[0]
    live_rows = padding[0]
    stream = patches[0]
    gathered = lax.all_gather(stream, "grp", axis=0, tiled=True)
    normed = normalize(gathered.astype(jnp.float32), first_gain, first_shift).astype(jnp.bfloat16)
    lifted = jnp.einsum("sd,dhe->she", normed, input_weight, preferred_element_type=jnp.float32)
    projected = (lifted + input_shift[None]).astype(jnp.bfloat16)
    mixed = attend(projected, segments, live_rows, head_dim)
    block = lax.optimization_barrier(mixed)
    attended = summed_apart(
        jnp.einsum("qhe,hed->qd", block, output_weight, preferred_element_type=jnp.float32).astype(
            jnp.bfloat16
        )
    )
    residual = (stream.astype(jnp.float32) + attended + output_shift).astype(jnp.bfloat16)
    normed_again = normalize(residual.astype(jnp.float32), second_gain, second_shift).astype(
        jnp.bfloat16
    )
    lifted = (
        jnp.dot(
            lax.all_gather(normed_again, "grp", axis=0, tiled=True),
            up_weight,
            preferred_element_type=jnp.float32,
        )
        + up_shift
    )
    activated = jax.nn.gelu(lifted, approximate=False).astype(jnp.bfloat16)
    block = lax.optimization_barrier(activated)
    fed = summed_apart(
        jnp.dot(block, down_weight, preferred_element_type=jnp.float32).astype(jnp.bfloat16)
    )
    layer_out = (residual.astype(jnp.float32) + fed + down_shift).astype(jnp.bfloat16)
    windows = layer_out.reshape(row_count // 4, 4 * model_width)
    merged = (
        jnp.dot(
            lax.all_gather(windows, "grp", axis=0, tiled=True),
            merge_weight,
            preferred_element_type=jnp.float32,
        )
        + merge_shift
    ).astype(jnp.bfloat16)
    outgoing = routed_rows(merged, segments, live_rows, request_owner[0])
    delivered = lax.all_to_all(outgoing, "tok", split_axis=0, concat_axis=0, tiled=True)
    return delivered[None]


def solution(mesh):
    return jax.shard_map(
        on_device,
        mesh=mesh,
        in_specs=(
            P("tok", "grp", None),
            P("tok", None),
            P("tok", None),
            P("tok", None),
            P(),
            P(),
            P(None, "grp", None),
            P("grp", None),
            P("grp", None, None),
            P(),
            P(),
            P(),
            P(None, "grp"),
            P("grp"),
            P("grp", None),
            P(),
            P(None, "grp"),
            P("grp"),
        ),
        out_specs=P("tok", None, None, "grp"),
        check_vma=False,
    )
```

profile of v0, /device:TPU:1, one launch (start us, length us, event | category | flops | bytes accessed | tf_op | source)
XLA Modules:
  0.0 143.6 jit_solution(7038068006779687679)
XLA Ops:
  0.0 27.2 %all-gather = bf16[1,256,1664]{2,1,0:T(8,128)(2,1)S(1)} all-gather(bf16[1,16,1664]{2,1,0:T(8,128)(2,1)} %param.18), channel_id=2, replica_groups=mesh['grp'=16,'tok'=32] {'grp'}, dimensions={1}, use_global_device_ids=true | all-gather | bytes 905216 | tf_op jit(solution)/shard_map/all_gather | solution.py:102
  27.2 0.2 convert_reduce_fusion
  27.5 0.4 fusion.3
  27.9 0.7 fusion.9
  28.6 0.3 fusion.50
  28.9 0.2 fusion.30
  29.1 0.1 fusion.32
  29.2 0.2 fusion.10
  29.4 0.2 copy-done.3
  29.6 0.4 convolution_convert_fusion.1
  30.1 27.0 %all_to_all.15 = bf16[16,16,1664]{2,1,0:T(8,128)(2,1)S(1)} all-to-all(bf16[16,16,1664]{2,1,0:T(8,128)(2,1)S(1)} %bitcast.72), channel_id=1, replica_groups=mesh['grp'=16,'tok'=32] {'grp'}, dimensions={0} | all-to-all | bytes 1703936 | tf_op jit(solution)/shard_map/all_to_all | solution.py:50
  57.1 0.1 convert_reduce_fusion.2
  57.3 0.1 convert_reduce_fusion.3
  57.4 0.2 fusion.35
  57.7 0.1 fusion.38
  57.7 16.8 %all_gather.10 = bf16[256,1664]{1,0:T(8,128)(2,1)S(1)} all-gather(bf16[16,1664]{1,0:T(8,128)(2,1)S(1)} %fusion.38), channel_id=1, replica_groups=mesh['grp'=16,'tok'=32] {'grp'}, dimensions={0}, use_global_device_ids=true | all-gather | bytes 905216 | tf_op jit(solution)/shard_map/all_gather | solution.py:119
  74.6 1.0 fusion.21
  75.6 0.2 copy-done.1
  75.7 1.4 convolution_convert_fusion
  77.1 5.3 %all-to-all-start.1 = ((bf16[16,16,1664]{2,1,0:T(8,128)(2,1)}), bf16[16,16,1664]{2,1,0:T(8,128)(2,1)S(1)}, u32[]{:S(2)}, u32[]{:S(2)}) async-start(bf16[16,16,1664]{2,1,0:T(8,128)(2,1)} %bitcast.17), calls=%async_computation.1 | async-start | bytes 1703936 | tf_op jit(solution)/shard_map/all_to_all | solution.py:50
  82.4 0.2 slice.15
  82.7 0.2 slice.16
  82.8 0.2 convert_reduce_fusion.4
  83.0 0.1 select_reduce_fusion
  83.2 23.3 %all-to-all-done.1 = bf16[16,16,1664]{2,1,0:T(8,128)(2,1)S(1)} async-done(((bf16[16,16,1664]{2,1,0:T(8,128)(2,1)}), bf16[16,16,1664]{2,1,0:T(8,128)(2,1)S(1)}, u32[]{:S(2)}, u32[]{:S(2)}) %all-to-all-start.1) | async-done | bytes 852000 | tf_op jit(solution)/shard_map/all_to_all | solution.py:50
  106.4 0.1 convert_reduce_fusion.1
  106.7 16.8 %all-gather.1 = bf16[16,4,6656]{2,1,0:T(4,128)(2,1)S(1)} all-gather(bf16[1,4,6656]{2,1,0:T(4,128)(2,1)S(1)} %fusion.43), channel_id=1, replica_groups=mesh['grp'=16,'tok'=32] {'grp'}, dimensions={0}, use_global_device_ids=true | all-gather | bytes 905216 | tf_op jit(solution)/shard_map/all_gather | solution.py:134
  123.5 0.2 reshape.122
  123.7 0.8 convolution_convert_fusion.2
  124.5 0.1 copy.26
  124.7 18.3 %all_to_all.16 = bf16[32,8,104]{2,1,0:T(8,128)(2,1)S(1)} all-to-all(bf16[32,8,104]{2,1,0:T(8,128)(2,1)S(1)} %bitcast.73), channel_id=1, replica_groups=mesh['grp'=16,'tok'=32] {'tok'}, dimensions={0} | all-to-all | bytes 106496 | tf_op jit(solution)/shard_map/all_to_all | solution.py:141
  143.0 0.6 copy.29
  (50 shorter events, 0.4 us)
Async XLA Ops:
  0.0 123.7 %copy-start = (bf16[6656,104]{0,1:T(8,128)(2,1)S(1)}, bf16[6656,104]{0,1:T(8,128)(2,1)}, u32[]{:S(2)}) copy-start(bf16[6656,104]{0,1:T(8,128)(2,1)} %param.34) | copy-start | bytes 4153348
  0.0 27.8 %copy-start.16 = (s32[1,256]{1,0:T(1,128)S(1)}, s32[1,256]{1,0:T(1,128)}, u32[]{:S(2)}) copy-start(s32[1,256]{1,0:T(1,128)} %param.20) | copy-start | bytes 3076
  0.0 27.9 %copy-start.9 = (f32[1,312]{1,0:T(1,128)S(1)}, f32[1,312]{1,0:T(1,128)}, u32[]{:S(2)}) copy-start(f32[1,312]{1,0:T(1,128)} %param.25) | copy-start | bytes 3748
  0.0 27.9 %copy-start.14 = (f32[1664]{0:T(1024)S(1)}, f32[1664]{0:T(1024)}, u32[]{:S(2)}) copy-start(f32[1664]{0:T(1024)} %param.22) | copy-start | bytes 19972
  0.0 27.9 %copy-start.13 = (f32[1664]{0:T(1024)S(1)}, f32[1664]{0:T(1024)}, u32[]{:S(2)}) copy-start(f32[1664]{0:T(1024)} %param.23) | copy-start | bytes 19972
  0.0 27.9 %copy-start.11 = (bf16[1664,1,312]{0,2,1:T(8,128)(2,1)S(1)}, bf16[1664,1,312]{0,2,1:T(8,128)(2,1)}, u32[]{:S(2)}) copy-start(bf16[1664,1,312]{0,2,1:T(8,128)(2,1)} %param.24) | copy-start | bytes 3115012
  27.9 0.7 copy-start.5
  28.6 1.0 copy-start.3
  30.0 27.2 %copy-start.2 = (bf16[1,16,1664]{2,1,0:T(8,128)(2,1)S(1)}, bf16[1,16,1664]{2,1,0:T(8,128)(2,1)}, u32[]{:S(2)}) copy-start(bf16[1,16,1664]{2,1,0:T(8,128)(2,1)} %param.18) | copy-start | bytes 159748
  30.1 27.2 %copy-start.4 = (f32[1664]{0:T(1024)S(1)}, f32[1664]{0:T(1024)}, u32[]{:S(2)}) copy-start(f32[1664]{0:T(1024)} %param.27) | copy-start | bytes 19972
  30.1 27.6 %copy-start.7 = (f32[1664]{0:T(1024)S(1)}, f32[1664]{0:T(1024)}, u32[]{:S(2)}) copy-start(f32[1664]{0:T(1024)} %param.29) | copy-start | bytes 19972
  30.1 27.6 %copy-start.8 = (f32[1664]{0:T(1024)S(1)}, f32[1664]{0:T(1024)}, u32[]{:S(2)}) copy-start(f32[1664]{0:T(1024)} %param.28) | copy-start | bytes 19972
  57.1 17.4 %copy-start.12 = (bf16[1664,256]{1,0:T(8,128)(2,1)S(1)}, bf16[1664,256]{1,0:T(8,128)(2,1)}, u32[]{:S(2)}) copy-start(bf16[1664,256]{1,0:T(8,128)(2,1)} %param.30) | copy-start | bytes 2555908
  57.1 17.4 %copy-start.15 = (f32[256]{0:T(256)S(1)}, f32[256]{0:T(256)}, u32[]{:S(2)}) copy-start(f32[256]{0:T(256)} %param.31) | copy-start | bytes 3076
  74.6 1.2 copy-start.1
  77.1 5.6 %copy-start.6 = (f32[1664]{0:T(1024)S(1)}, f32[1664]{0:T(1024)}, u32[]{:S(2)}) copy-start(f32[1664]{0:T(1024)} %param.33) | copy-start | bytes 19972
  77.1 5.9 %copy-start.17 = (s32[1,32]{1,0:T(1,128)S(1)}, s32[1,32]{1,0:T(1,128)}, u32[]{:S(2)}) copy-start(s32[1,32]{1,0:T(1,128)} %param.21) | copy-start | bytes 388
  77.1 29.4 %all-to-all-start.1 = ((bf16[16,16,1664]{2,1,0:T(8,128)(2,1)}), bf16[16,16,1664]{2,1,0:T(8,128)(2,1)S(1)}, u32[]{:S(2)}, u32[]{:S(2)}) async-start(bf16[16,16,1664]{2,1,0:T(8,128)(2,1)} %bitcast.17), calls=%async_computation.1 | async-start | bytes 1703936 | tf_op jit(solution)/shard_map/all_to_all | solution.py:50
  106.7 17.0 %copy-start.10 = (f32[104]{0:T(128)S(1)}, f32[104]{0:T(128)}, u32[]{:S(2)}) copy-start(f32[104]{0:T(128)} %param.35) | copy-start | bytes 1252
where the time goes:
time: 144 us
  blocking collectives  106 us (74%)
  waiting for transfers between devices  23.3 us (16%)
  starting transfers between devices  5.33 us (4%)
  matrix products  4.68 us (3%)
  other arithmetic  1.96 us (1%)
  local copies, waits for them, and re-layouts  1.85 us (1%)
    all_gather x1, blocking collectives, on_device(): gathered = lax.all_gather(stream, 'grp', axis=0, tiled=True)  27.2 us
    all_to_all x1, blocking collectives, summed_apart(): lax.all_to_all(terms.reshape(shards, rows, terms.shape[1]), 'grp', 0, 0,...  27 us
    all_to_all x1, waiting for transfers between devices, summed_apart(): lax.all_to_all(terms.reshape(shards, rows, terms.shape[1]), 'grp', 0, 0,...  23.3 us
    all_to_all x1, blocking collectives, on_device(): lax.all_to_all(outgoing, 'tok', split_axis=0, concat_axis=0, tiled=True)  18.3 us
    all_gather x1, blocking collectives, on_device(): lax.all_gather(windows, 'grp', axis=0, tiled=True)  16.8 us
    all_gather x1, blocking collectives, on_device(): lax.all_gather(normed_again, 'grp', axis=0, tiled=True)  16.8 us
    all_to_all x1, starting transfers between devices, summed_apart(): lax.all_to_all(terms.reshape(shards, rows, terms.shape[1]), 'grp', 0, 0,...  5.33 us
  transfers between devices with their start and end apart: 1, of which 1 were waited for; matrix products, arithmetic and copies ran while one was open for 0% of the time, Pallas kernels for 0%

commit v1 on v0

--- a/solution.py
+++ b/solution.py
@@ -5,6 +5,24 @@
 
 CAP = 8
 epsilon = 1e-06
+
+
+def post_numbers_now(work_x):
+    many = lax.axis_size("grp")
+    pages = []
+    for d in range(many):
+        pages.append((d, (d + 1) % many))
+    table = []
+    for d in range(many):
+        table.append((d, (d - 1) % many))
+    vec_out, low = ([work_x], [work_x])
+    for _ in range(many // 2):
+        vec_out.append(lax.ppermute(vec_out[-1], axis_name="grp", perm=pages))
+    for _ in range((many - 1) // 2):
+        low.append(lax.ppermute(low[-1], perm=table, axis_name="grp"))
+    inter = jnp.concatenate([*vec_out[::-1], *low[1:]], axis=0)
+    now = jnp.roll(inter, (lax.axis_index("grp") - many // 2) * work_x.shape[0], 0)
+    return now
 
 
 def normalize(stream, factor, adjust):
@@ -99,7 +117,7 @@
     segments = segment_ids[0]
     live_rows = padding[0]
     stream = patches[0]
-    gathered = lax.all_gather(stream, "grp", axis=0, tiled=True)
+    gathered = post_numbers_now(stream)
     normed = normalize(gathered.astype(jnp.float32), first_gain, first_shift).astype(jnp.bfloat16)
     lifted = jnp.einsum("sd,dhe->she", normed, input_weight, preferred_element_type=jnp.float32)
     projected = (lifted + input_shift[None]).astype(jnp.bfloat16)

time: 144 us -> 166 us (1.15)
  starting transfers between devices: 5.33 us -> 36.4 us
  blocking collectives: 106 us -> 84.9 us
  waiting for transfers between devices: 23.3 us -> 32.7 us
    ppermute x0 -> x15, starting transfers between devices: none -> 31.2 us  [the longest x7 27.7 us: post_numbers_now(): low.append(lax.ppermute(low[-1], perm=table, axis_name='grp'))]
    all_gather x1 -> x0, blocking collectives: 27.2 us -> none  [on_device(): gathered = lax.all_gather(stream, 'grp', axis=0, tiled=True)]
    ppermute x0 -> x15, waiting for transfers between devices: none -> 9.48 us  [the longest x8 7.64 us: post_numbers_now(): vec_out.append(lax.ppermute(vec_out[-1], axis_name='grp', perm=pages))]
    all_to_all x1, blocking collectives: 27 us -> 32.9 us  [summed_apart(): lax.all_to_all(terms.reshape(shards, rows, terms.shape[1]), 'grp', 0, 0,...]
  transfers between devices with their start and end apart: 1 -> 16, of which waited for: 1 -> 13; matrix products, arithmetic and copies ran while one was open for 0% -> 2% of each run, Pallas kernels for 0% -> 0%
where the time goes in v1:
time: 166 us
  blocking collectives  84.9 us (51%)
  starting transfers between devices  36.4 us (22%)
  waiting for transfers between devices  32.7 us (20%)
  matrix products  4.66 us (3%)
  local copies, waits for them, and re-layouts  3.37 us (2%)
  other arithmetic  3.32 us (2%)
    all_to_all x1, blocking collectives, summed_apart(): lax.all_to_all(terms.reshape(shards, rows, terms.shape[1]), 'grp', 0, 0,...  32.9 us
    ppermute x7, starting transfers between devices, post_numbers_now(): low.append(lax.ppermute(low[-1], perm=table, axis_name='grp'))  27.7 us
    all_to_all x1, waiting for transfers between devices, summed_apart(): lax.all_to_all(terms.reshape(shards, rows, terms.shape[1]), 'grp', 0, 0,...  23.3 us
    all_to_all x1, blocking collectives, on_device(): lax.all_to_all(outgoing, 'tok', split_axis=0, concat_axis=0, tiled=True)  18.3 us
    all_gather x1, blocking collectives, on_device(): lax.all_gather(windows, 'grp', axis=0, tiled=True)  16.8 us
    all_gather x1, blocking collectives, on_device(): lax.all_gather(normed_again, 'grp', axis=0, tiled=True)  16.8 us
    ppermute x8, waiting for transfers between devices, post_numbers_now(): vec_out.append(lax.ppermute(vec_out[-1], axis_name='grp', perm=pages))  7.64 us
    all_to_all x1, starting transfers between devices, summed_apart(): lax.all_to_all(terms.reshape(shards, rows, terms.shape[1]), 'grp', 0, 0,...  5.2 us
  transfers between devices with their start and end apart: 16, of which 13 were waited for; matrix products, arithmetic and copies ran while one was open for 2% of the time, Pallas kernels for 0%

profile of v1, /device:TPU:1, one launch (start us, length us, event | category | flops | bytes accessed | tf_op | source)
XLA Modules:
  0.0 165.8 jit_solution(6201732892548366074)
XLA Ops:
  0.0 3.5 %collective-permute-start = (bf16[16,1664]{1,0:T(8,128)(2,1)}, bf16[16,1664]{1,0:T(8,128)(2,1)S(1)}, u32[]{:S(2)}, u32[]{:S(2)}) collective-permute-start(bf16[16,1664]{1,0:T(8,128)(2,1)} %bitcast.54), channel_id=1, source_target_pairs={{0,32},{32,64},{64,96},{96,128},{128,160},{160,192},{192,224},{224... | collective-permute-start | bytes 159752 | tf_op jit(solution)/shard_map/ppermute | solution.py:20
  3.5 4.3 %collective-permute-done = bf16[16,1664]{1,0:T(8,128)(2,1)S(1)} collective-permute-done((bf16[16,1664]{1,0:T(8,128)(2,1)}, bf16[16,1664]{1,0:T(8,128)(2,1)S(1)}, u32[]{:S(2)}, u32[]{:S(2)}) %collective-permute-start) | collective-permute-done | bytes 53280 | tf_op jit(solution)/shard_map/ppermute | solution.py:20
  7.8 4.3 %collective-permute-start.8 = (bf16[16,1664]{1,0:T(8,128)(2,1)}, bf16[16,1664]{1,0:T(8,128)(2,1)S(1)}, u32[]{:S(2)}, u32[]{:S(2)}) collective-permute-start(bf16[16,1664]{1,0:T(8,128)(2,1)} %bitcast.55), channel_id=1, source_target_pairs={{0,480},{32,0},{64,32},{96,64},{128,96},{160,128},{192,160},{224,1... | collective-permute-start | bytes 159752 | tf_op jit(solution)/shard_map/ppermute | solution.py:22
  12.0 0.7 collective-permute-done.1
  12.8 0.4 collective-permute-done.8
  13.1 4.0 %collective-permute-start.9 = (bf16[16,1664]{1,0:T(8,128)(2,1)S(1)}, bf16[16,1664]{1,0:T(8,128)(2,1)S(1)}, u32[]{:S(2)}, u32[]{:S(2)}) collective-permute-start(bf16[16,1664]{1,0:T(8,128)(2,1)S(1)} %collective-permute-done.8), channel_id=1, source_target_pairs={{0,480},{32,0},{64,32},{96,64},{128,96},{160,128},{192,160},{224,1... | collective-permute-start | bytes 159752 | tf_op jit(solution)/shard_map/ppermute | solution.py:22
  17.1 0.4 collective-permute-done.2
  17.5 0.4 collective-permute-done.9
  18.0 3.8 %collective-permute-start.10 = (bf16[16,1664]{1,0:T(8,128)(2,1)S(1)}, bf16[16,1664]{1,0:T(8,128)(2,1)S(1)}, u32[]{:S(2)}, u32[]{:S(2)}) collective-permute-start(bf16[16,1664]{1,0:T(8,128)(2,1)S(1)} %collective-permute-done.9), channel_id=1, source_target_pairs={{0,480},{32,0},{64,32},{96,64},{128,96},{160,128},{192,160},{224,1... | collective-permute-start | bytes 159752 | tf_op jit(solution)/shard_map/ppermute | solution.py:22
  21.8 0.5 collective-permute-done.3
  22.7 3.9 %collective-permute-start.11 = (bf16[16,1664]{1,0:T(8,128)(2,1)S(1)}, bf16[16,1664]{1,0:T(8,128)(2,1)S(1)}, u32[]{:S(2)}, u32[]{:S(2)}) collective-permute-start(bf16[16,1664]{1,0:T(8,128)(2,1)S(1)} %collective-permute-done.10), channel_id=1, source_target_pairs={{0,480},{32,0},{64,32},{96,64},{128,96},{160,128},{192,160},{224,1... | collective-permute-start | bytes 159752 | tf_op jit(solution)/shard_map/ppermute | solution.py:22
  26.5 0.5 collective-permute-done.4
  27.4 3.9 %collective-permute-start.12 = (bf16[16,1664]{1,0:T(8,128)(2,1)S(1)}, bf16[16,1664]{1,0:T(8,128)(2,1)S(1)}, u32[]{:S(2)}, u32[]{:S(2)}) collective-permute-start(bf16[16,1664]{1,0:T(8,128)(2,1)S(1)} %collective-permute-done.11), channel_id=1, source_target_pairs={{0,480},{32,0},{64,32},{96,64},{128,96},{160,128},{192,160},{224,1... | collective-permute-start | bytes 159752 | tf_op jit(solution)/shard_map/ppermute | solution.py:22
  31.3 0.5 collective-permute-done.5
  32.2 3.9 %collective-permute-start.13 = (bf16[16,1664]{1,0:T(8,128)(2,1)S(1)}, bf16[16,1664]{1,0:T(8,128)(2,1)S(1)}, u32[]{:S(2)}, u32[]{:S(2)}) collective-permute-start(bf16[16,1664]{1,0:T(8,128)(2,1)S(1)} %collective-permute-done.12), channel_id=1, source_target_pairs={{0,480},{32,0},{64,32},{96,64},{128,96},{160,128},{192,160},{224,1... | collective-permute-start | bytes 159752 | tf_op jit(solution)/shard_map/ppermute | solution.py:22
  36.1 0.5 collective-permute-done.6
  36.6 0.7 compare_reduce_fusion
  37.3 0.7 reduce.4
  38.1 4.1 %collective-permute-start.14 = (bf16[16,1664]{1,0:T(8,128)(2,1)S(1)}, bf16[16,1664]{1,0:T(8,128)(2,1)S(1)}, u32[]{:S(2)}, u32[]{:S(2)}) collective-permute-start(bf16[16,1664]{1,0:T(8,128)(2,1)S(1)} %collective-permute-done.13), channel_id=1, source_target_pairs={{0,480},{32,0},{64,32},{96,64},{128,96},{160,128},{192,160},{224,1... | collective-permute-start | bytes 159752 | tf_op jit(solution)/shard_map/ppermute | solution.py:22
  42.2 0.8 constant_dynamic-update-slice_fusion.23
  44.4 0.7 fusion.8
  46.0 0.4 convolution_convert_fusion.1
  46.5 32.9 %all_to_all.15 = bf16[16,16,1664]{2,1,0:T(8,128)(2,1)S(1)} all-to-all(bf16[16,16,1664]{2,1,0:T(8,128)(2,1)S(1)} %bitcast.53), channel_id=1, replica_groups=mesh['grp'=16,'tok'=32] {'grp'}, dimensions={0} | all-to-all | bytes 1703936 | tf_op jit(solution)/shard_map/all_to_all | solution.py:68
  80.0 16.8 %all_gather.6 = bf16[256,1664]{1,0:T(8,128)(2,1)S(1)} all-gather(bf16[16,1664]{1,0:T(8,128)(2,1)S(1)} %fusion.38), channel_id=1, replica_groups=mesh['grp'=16,'tok'=32] {'grp'}, dimensions={0}, use_global_device_ids=true | all-gather | bytes 905216 | tf_op jit(solution)/shard_map/all_gather | solution.py:137
  96.8 1.0 fusion.21
  98.0 1.3 convolution_convert_fusion
  99.3 5.2 %all-to-all-start.1 = ((bf16[16,16,1664]{2,1,0:T(8,128)(2,1)}), bf16[16,16,1664]{2,1,0:T(8,128)(2,1)S(1)}, u32[]{:S(2)}, u32[]{:S(2)}) async-start(bf16[16,16,1664]{2,1,0:T(8,128)(2,1)} %bitcast.16), calls=%async_computation.1 | async-start | bytes 1703936 | tf_op jit(solution)/shard_map/all_to_all | solution.py:68
  105.3 23.3 %all-to-all-done.1 = bf16[16,16,1664]{2,1,0:T(8,128)(2,1)S(1)} async-done(((bf16[16,16,1664]{2,1,0:T(8,128)(2,1)}), bf16[16,16,1664]{2,1,0:T(8,128)(2,1)S(1)}, u32[]{:S(2)}, u32[]{:S(2)}) %all-to-all-start.1) | async-done | bytes 852000 | tf_op jit(solution)/shard_map/all_to_all | solution.py:68
  128.8 16.8 %all-gather = bf16[16,4,6656]{2,1,0:T(4,128)(2,1)S(1)} all-gather(bf16[1,4,6656]{2,1,0:T(4,128)(2,1)S(1)} %fusion.41), channel_id=1, replica_groups=mesh['grp'=16,'tok'=32] {'grp'}, dimensions={0}, use_global_device_ids=true | all-gather | bytes 905216 | tf_op jit(solution)/shard_map/all_gather | solution.py:152
  145.9 0.8 convolution_convert_fusion.2
  146.8 18.3 %all_to_all.16 = bf16[32,8,104]{2,1,0:T(8,128)(2,1)S(1)} all-to-all(bf16[32,8,104]{2,1,0:T(8,128)(2,1)S(1)} %bitcast.56), channel_id=1, replica_groups=mesh['grp'=16,'tok'=32] {'tok'}, dimensions={0} | all-to-all | bytes 106496 | tf_op jit(solution)/shard_map/all_to_all | solution.py:159
  165.1 0.6 copy.60
  (109 shorter events, 5.3 us)
Async XLA Ops:
  0.0 145.9 %copy-start = (bf16[6656,104]{0,1:T(8,128)(2,1)S(1)}, bf16[6656,104]{0,1:T(8,128)(2,1)}, u32[]{:S(2)}) copy-start(bf16[6656,104]{0,1:T(8,128)(2,1)} %param.34) | copy-start | bytes 4153348
  0.0 43.3 %copy-start.2 = (bf16[1,16,1664]{2,1,0:T(8,128)(2,1)S(1)}, bf16[1,16,1664]{2,1,0:T(8,128)(2,1)}, u32[]{:S(2)}) copy-start(bf16[1,16,1664]{2,1,0:T(8,128)(2,1)} %param.18) | copy-start | bytes 159748
  0.0 7.8 %collective-permute-start = (bf16[16,1664]{1,0:T(8,128)(2,1)}, bf16[16,1664]{1,0:T(8,128)(2,1)S(1)}, u32[]{:S(2)}, u32[]{:S(2)}) collective-permute-start(bf16[16,1664]{1,0:T(8,128)(2,1)} %bitcast.54), channel_id=1, source_target_pairs={{0,32},{32,64},{64,96},{96,128},{128,160},{160,192},{192,224},{224... | collective-permute-start | bytes 159752 | tf_op jit(solution)/shard_map/ppermute | solution.py:20
  7.8 5.0 %collective-permute-start.1 = (bf16[16,1664]{1,0:T(8,128)(2,1)S(1)}, bf16[16,1664]{1,0:T(8,128)(2,1)S(1)}, u32[]{:S(2)}, u32[]{:S(2)}) collective-permute-start(bf16[16,1664]{1,0:T(8,128)(2,1)S(1)} %collective-permute-done), channel_id=1, source_target_pairs={{0,32},{32,64},{64,96},{96,128},{128,160},{160,192},{192,224},{224... | collective-permute-start | bytes 159752 | tf_op jit(solution)/shard_map/ppermute | solution.py:20
  7.8 5.4 %collective-permute-start.8 = (bf16[16,1664]{1,0:T(8,128)(2,1)}, bf16[16,1664]{1,0:T(8,128)(2,1)S(1)}, u32[]{:S(2)}, u32[]{:S(2)}) collective-permute-start(bf16[16,1664]{1,0:T(8,128)(2,1)} %bitcast.55), channel_id=1, source_target_pairs={{0,480},{32,0},{64,32},{96,64},{128,96},{160,128},{192,160},{224,1... | collective-permute-start | bytes 159752 | tf_op jit(solution)/shard_map/ppermute | solution.py:22
  12.8 4.8 %collective-permute-start.2 = (bf16[16,1664]{1,0:T(8,128)(2,1)S(1)}, bf16[16,1664]{1,0:T(8,128)(2,1)S(1)}, u32[]{:S(2)}, u32[]{:S(2)}) collective-permute-start(bf16[16,1664]{1,0:T(8,128)(2,1)S(1)} %collective-permute-done.1), channel_id=1, source_target_pairs={{0,32},{32,64},{64,96},{96,128},{128,160},{160,192},{192,224},{224... | collective-permute-start | bytes 159752 | tf_op jit(solution)/shard_map/ppermute | solution.py:20
  13.1 4.8 %collective-permute-start.9 = (bf16[16,1664]{1,0:T(8,128)(2,1)S(1)}, bf16[16,1664]{1,0:T(8,128)(2,1)S(1)}, u32[]{:S(2)}, u32[]{:S(2)}) collective-permute-start(bf16[16,1664]{1,0:T(8,128)(2,1)S(1)} %collective-permute-done.8), channel_id=1, source_target_pairs={{0,480},{32,0},{64,32},{96,64},{128,96},{160,128},{192,160},{224,1... | collective-permute-start | bytes 159752 | tf_op jit(solution)/shard_map/ppermute | solution.py:22
  17.5 4.8 %collective-permute-start.3 = (bf16[16,1664]{1,0:T(8,128)(2,1)S(1)}, bf16[16,1664]{1,0:T(8,128)(2,1)S(1)}, u32[]{:S(2)}, u32[]{:S(2)}) collective-permute-start(bf16[16,1664]{1,0:T(8,128)(2,1)S(1)} %collective-permute-done.2), channel_id=1, source_target_pairs={{0,32},{32,64},{64,96},{96,128},{128,160},{160,192},{192,224},{224... | collective-permute-start | bytes 159752 | tf_op jit(solution)/shard_map/ppermute | solution.py:20
  18.0 4.7 %collective-permute-start.10 = (bf16[16,1664]{1,0:T(8,128)(2,1)S(1)}, bf16[16,1664]{1,0:T(8,128)(2,1)S(1)}, u32[]{:S(2)}, u32[]{:S(2)}) collective-permute-start(bf16[16,1664]{1,0:T(8,128)(2,1)S(1)} %collective-permute-done.9), channel_id=1, source_target_pairs={{0,480},{32,0},{64,32},{96,64},{128,96},{160,128},{192,160},{224,1... | collective-permute-start | bytes 159752 | tf_op jit(solution)/shard_map/ppermute | solution.py:22
  22.3 4.8 %collective-permute-start.4 = (bf16[16,1664]{1,0:T(8,128)(2,1)S(1)}, bf16[16,1664]{1,0:T(8,128)(2,1)S(1)}, u32[]{:S(2)}, u32[]{:S(2)}) collective-permute-start(bf16[16,1664]{1,0:T(8,128)(2,1)S(1)} %collective-permute-done.3), channel_id=1, source_target_pairs={{0,32},{32,64},{64,96},{96,128},{128,160},{160,192},{192,224},{224... | collective-permute-start | bytes 159752 | tf_op jit(solution)/shard_map/ppermute | solution.py:20
  22.7 4.8 %collective-permute-start.11 = (bf16[16,1664]{1,0:T(8,128)(2,1)S(1)}, bf16[16,1664]{1,0:T(8,128)(2,1)S(1)}, u32[]{:S(2)}, u32[]{:S(2)}) collective-permute-start(bf16[16,1664]{1,0:T(8,128)(2,1)S(1)} %collective-permute-done.10), channel_id=1, source_target_pairs={{0,480},{32,0},{64,32},{96,64},{128,96},{160,128},{192,160},{224,1... | collective-permute-start | bytes 159752 | tf_op jit(solution)/shard_map/ppermute | solution.py:22
  27.1 4.8 %collective-permute-start.5 = (bf16[16,1664]{1,0:T(8,128)(2,1)S(1)}, bf16[16,1664]{1,0:T(8,128)(2,1)S(1)}, u32[]{:S(2)}, u32[]{:S(2)}) collective-permute-start(bf16[16,1664]{1,0:T(8,128)(2,1)S(1)} %collective-permute-done.4), channel_id=1, source_target_pairs={{0,32},{32,64},{64,96},{96,128},{128,160},{160,192},{192,224},{224... | collective-permute-start | bytes 159752 | tf_op jit(solution)/shard_map/ppermute | solution.py:20
  27.4 4.8 %collective-permute-start.12 = (bf16[16,1664]{1,0:T(8,128)(2,1)S(1)}, bf16[16,1664]{1,0:T(8,128)(2,1)S(1)}, u32[]{:S(2)}, u32[]{:S(2)}) collective-permute-start(bf16[16,1664]{1,0:T(8,128)(2,1)S(1)} %collective-permute-done.11), channel_id=1, source_target_pairs={{0,480},{32,0},{64,32},{96,64},{128,96},{160,128},{192,160},{224,1... | collective-permute-start | bytes 159752 | tf_op jit(solution)/shard_map/ppermute | solution.py:22
  31.9 4.8 %collective-permute-start.6 = (bf16[16,1664]{1,0:T(8,128)(2,1)S(1)}, bf16[16,1664]{1,0:T(8,128)(2,1)S(1)}, u32[]{:S(2)}, u32[]{:S(2)}) collective-permute-start(bf16[16,1664]{1,0:T(8,128)(2,1)S(1)} %collective-permute-done.5), channel_id=1, source_target_pairs={{0,32},{32,64},{64,96},{96,128},{128,160},{160,192},{192,224},{224... | collective-permute-start | bytes 159752 | tf_op jit(solution)/shard_map/ppermute | solution.py:20
  32.2 5.9 %collective-permute-start.13 = (bf16[16,1664]{1,0:T(8,128)(2,1)S(1)}, bf16[16,1664]{1,0:T(8,128)(2,1)S(1)}, u32[]{:S(2)}, u32[]{:S(2)}) collective-permute-start(bf16[16,1664]{1,0:T(8,128)(2,1)S(1)} %collective-permute-done.12), channel_id=1, source_target_pairs={{0,480},{32,0},{64,32},{96,64},{128,96},{160,128},{192,160},{224,1... | collective-permute-start | bytes 159752 | tf_op jit(solution)/shard_map/ppermute | solution.py:22
  36.6 5.5 %collective-permute-start.7 = (bf16[16,1664]{1,0:T(8,128)(2,1)S(1)}, bf16[16,1664]{1,0:T(8,128)(2,1)S(1)}, u32[]{:S(2)}, u32[]{:S(2)}) collective-permute-start(bf16[16,1664]{1,0:T(8,128)(2,1)S(1)} %collective-permute-done.6), channel_id=1, source_target_pairs={{0,32},{32,64},{64,96},{96,128},{128,160},{160,192},{192,224},{224... | collective-permute-start | bytes 159752 | tf_op jit(solution)/shard_map/ppermute | solution.py:20
  38.1 5.1 %collective-permute-start.14 = (bf16[16,1664]{1,0:T(8,128)(2,1)S(1)}, bf16[16,1664]{1,0:T(8,128)(2,1)S(1)}, u32[]{:S(2)}, u32[]{:S(2)}) collective-permute-start(bf16[16,1664]{1,0:T(8,128)(2,1)S(1)} %collective-permute-done.13), channel_id=1, source_target_pairs={{0,480},{32,0},{64,32},{96,64},{128,96},{160,128},{192,160},{224,1... | collective-permute-start | bytes 159752 | tf_op jit(solution)/shard_map/ppermute | solution.py:22
  43.2 1.2 copy-start.10
  43.2 1.2 copy-start.12
  43.2 1.2 copy-start.13
  45.1 1.0 copy-start.3
  46.0 33.5 %copy-start.4 = (f32[1664]{0:T(1024)S(1)}, f32[1664]{0:T(1024)}, u32[]{:S(2)}) copy-start(f32[1664]{0:T(1024)} %param.27) | copy-start | bytes 19972
  46.5 33.4 %copy-start.7 = (f32[1664]{0:T(1024)S(1)}, f32[1664]{0:T(1024)}, u32[]{:S(2)}) copy-start(f32[1664]{0:T(1024)} %param.29) | copy-start | bytes 19972
  46.5 33.4 %copy-start.8 = (f32[1664]{0:T(1024)S(1)}, f32[1664]{0:T(1024)}, u32[]{:S(2)}) copy-start(f32[1664]{0:T(1024)} %param.28) | copy-start | bytes 19972
  46.5 50.3 %copy-start.11 = (bf16[1664,256]{1,0:T(8,128)(2,1)S(1)}, bf16[1664,256]{1,0:T(8,128)(2,1)}, u32[]{:S(2)}) copy-start(bf16[1664,256]{1,0:T(8,128)(2,1)} %param.30) | copy-start | bytes 2555908
  46.5 50.3 %copy-start.14 = (f32[256]{0:T(256)S(1)}, f32[256]{0:T(256)}, u32[]{:S(2)}) copy-start(f32[256]{0:T(256)} %param.31) | copy-start | bytes 3076
  96.8 1.2 copy-start.1
  98.0 6.8 %copy-start.6 = (f32[1664]{0:T(1024)S(1)}, f32[1664]{0:T(1024)}, u32[]{:S(2)}) copy-start(f32[1664]{0:T(1024)} %param.33) | copy-start | bytes 19972
  98.0 6.8 %copy-start.15 = (s32[1,256]{1,0:T(1,128)S(1)}, s32[1,256]{1,0:T(1,128)}, u32[]{:S(2)}) copy-start(s32[1,256]{1,0:T(1,128)} %param.20) | copy-start | bytes 3076
  98.0 7.2 %copy-start.16 = (s32[1,32]{1,0:T(1,128)S(1)}, s32[1,32]{1,0:T(1,128)}, u32[]{:S(2)}) copy-start(s32[1,32]{1,0:T(1,128)} %param.21) | copy-start | bytes 388
  99.3 29.2 %all-to-all-start.1 = ((bf16[16,16,1664]{2,1,0:T(8,128)(2,1)}), bf16[16,16,1664]{2,1,0:T(8,128)(2,1)S(1)}, u32[]{:S(2)}, u32[]{:S(2)}) async-start(bf16[16,16,1664]{2,1,0:T(8,128)(2,1)} %bitcast.16), calls=%async_computation.1 | async-start | bytes 1703936 | tf_op jit(solution)/shard_map/all_to_all | solution.py:68
  128.7 17.2 %copy-start.9 = (f32[104]{0:T(128)S(1)}, f32[104]{0:T(128)}, u32[]{:S(2)}) copy-start(f32[104]{0:T(128)} %param.35) | copy-start | bytes 1252
  (1 other events, 0.7 us)
